TPU v7x, 256 devices: a whole 4x4x8 slice. The times are simulated.
256 devices in a mesh: ctx: 64 (over z, x_hi, y), hd: 4 (over x_lo, core).
Axes of the slice: x: 4 (x_hi: 2, x_lo: 2; x = x_hi * 2 + x_lo), y: 4, z: 8, core: 2. Of those that a mesh axis runs over, the one named last changes fastest.
Arguments:
- tokens: bfloat16 [32768, 4096], P('ctx'), may hold values from -6 to 6
- w_query: bfloat16 [4096, 2048], P('ctx', 'hd'), may hold values from -0.09375 to 0.09375
- w_key: bfloat16 [4096, 2048], P('ctx', 'hd'), may hold values from -0.09375 to 0.09375
- w_value: bfloat16 [4096, 2048], P('ctx', 'hd'), may hold values from -0.09375 to 0.09375
Outputs:
- attended: bfloat16 [32768, 2048], P('ctx', 'hd')
All inputs are finite; a program needn't handle non-finite values.
Results may differ from a plain program's by a relative error of at most 0.0065.
Values may be sent and summed in bfloat16 or wider, within the bound.
No kernel may reach another device: no remote copies, remote signals or barrier semaphores. Data moves between devices by JAX's collectives and lax.ppermute only.
A program may use at most 64 MiB of HBM per device.

v0:
```python
import jax
import jax.numpy as jnp
from jax import lax
from jax.sharding import PartitionSpec as P

DH = 128
BLOCK = 512
epsilon = 1e-06


def carried_in(part, axis, combine, identity):
    place = lax.axis_index(axis)
    gathered = lax.all_gather(part, axis)
    state = jnp.zeros_like(part) + jnp.asarray(identity, part.dtype)

    def one(hop, state):
        return combine(state, lax.dynamic_index_in_dim(gathered, hop, 0, False))

    return lax.fori_loop(0, place, one, state)


def local(tokens, w_query, w_key, w_value):
    tok_rows = tokens.shape[0]
    width_group = w_query.shape[1]
    head_count = width_group // DH
    block_count = tok_rows // BLOCK
    query_full = jnp.dot(
        tokens,
        lax.all_gather(w_query, "ctx", axis=0, tiled=True),
        preferred_element_type=jnp.float32,
    )
    key_full = jnp.dot(
        tokens, lax.all_gather(w_key, "ctx", axis=0, tiled=True), preferred_element_type=jnp.float32
    )
    value_full = jnp.dot(
        tokens,
        lax.all_gather(w_value, "ctx", axis=0, tiled=True),
        preferred_element_type=jnp.float32,
    )
    query_rows = query_full.astype(jnp.bfloat16).reshape(block_count, BLOCK, head_count, DH)
    key_rows = key_full.astype(jnp.bfloat16).reshape(block_count, BLOCK, head_count, DH)
    value_rows = value_full.astype(jnp.bfloat16).reshape(block_count, BLOCK, head_count, DH)
    causal_mask = jnp.tril(jnp.ones((BLOCK, BLOCK), dtype=bool))
    scores = jnp.einsum("bqhd,bkhd->bhqk", query_rows, key_rows, preferred_element_type=jnp.float32)
    scores = jnp.where(causal_mask[None, None], scores, 0.0).astype(jnp.bfloat16)
    local_term = jnp.einsum(
        "bhqk,bkhd->bqhd", scores, value_rows, preferred_element_type=jnp.float32
    )
    block_states = jnp.einsum(
        "bkhd,bkhe->bhde", key_rows, value_rows, preferred_element_type=jnp.float32
    )
    own_total = jnp.sum(block_states, axis=0)

    def add_states(earlier, later_part):
        return earlier + later_part

    prefix_state = carried_in(own_total, "ctx", add_states, jnp.zeros_like(own_total))
    before_blocks = jnp.concatenate([jnp.zeros_like(block_states), block_states[:-1]], axis=0)
    start_states = prefix_state[None] + jnp.cumsum(before_blocks, axis=0)
    carried = jnp.einsum(
        "bqhd,bhde->bqhe",
        query_rows.astype(jnp.float32),
        start_states,
        precision=lax.Precision.HIGHEST,
    )
    attended_raw = carried + local_term
    scale_inv = lax.rsqrt(jnp.mean(attended_raw * attended_raw, axis=-1, keepdims=True) + epsilon)
    return (attended_raw * scale_inv).astype(jnp.bfloat16).reshape(tok_rows, width_group)


def solution(mesh):
    return jax.shard_map(
        local,
        mesh=mesh,
        in_specs=(P("ctx", None), P("ctx", "hd"), P("ctx", "hd"), P("ctx", "hd")),
        out_specs=P("ctx", "hd"),
        check_vma=False,
    )
```

profile of v0, /device:TPU:254, one launch (start us, length us, event | category | flops | bytes accessed | tf_op | source)
XLA Modules:
  0.0 674.8 jit_solution(13655943641388664750)
XLA Ops:
  8.8 126.3 %all-gather.6.cloned.1.call-done = bf16[4096,512]{1,0:T(8,128)(2,1)} async-done(((bf16[64,512]{1,0:T(8,128)(2,1)}), bf16[4096,512]{1,0:T(8,128)(2,1)}) %all-gather.6.cloned.1.call-update) | async-done | bytes 4194320 | tf_op jit(solution)/shard_map/all_gather | solution.py:33
  135.0 5.8 convolution_convert_fusion.2
  140.9 121.8 %all-gather.8.cloned.1.call-done = bf16[4096,512]{1,0:T(8,128)(2,1)} async-done(((bf16[64,512]{1,0:T(8,128)(2,1)}), bf16[4096,512]{1,0:T(8,128)(2,1)}) %all-gather.8.cloned.1.call-update) | async-done | bytes 4194320 | tf_op jit(solution)/shard_map/all_gather | solution.py:37
  262.7 5.8 convolution_convert_fusion.1
  270.5 119.9 %all-gather.10.cloned.1.call-done = bf16[4096,512]{1,0:T(8,128)(2,1)} async-done(((bf16[64,512]{1,0:T(8,128)(2,1)}), bf16[4096,512]{1,0:T(8,128)(2,1)}) %all-gather.10.cloned.1.call-update) | async-done | bytes 4194320 | tf_op jit(solution)/shard_map/all_gather | solution.py:29
  390.4 5.8 convolution_convert_fusion
  396.2 202.4 %all-gather.12.cloned.1.call-done = f32[256,128,128]{2,1,0:T(8,128)} async-done(((f32[4,128,128]{2,1,0:T(8,128)}), f32[256,128,128]{2,1,0:T(8,128)}) %all-gather.12.cloned.1.call-update) | async-done | bytes 16777232 | tf_op jit(solution)/shard_map/all_gather | solution.py:13
  598.6 65.4 %while.10 = (s32[]{:T(128)}, f32[4,128,128]{2,1,0:T(8,128)S(1)}, s32[]{:T(128)}, f32[64,4,128,128]{3,2,1,0:T(8,128)}, s32[]{:T(128)}, /*index=5*/s32[]{:T(128)}, s32[]{:T(128)}) while((s32[]{:T(128)}, f32[4,128,128]{2,1,0:T(8,128)S(1)}, s32[]{:T(128)}, f32[64,4,128,128]{3,2,1,0:T(8,128)}, s32[]{:T(128)}, /*index=5*/s32[]{:T(128)}, ...), condition=%wide.region_1.2_spmd, body=%wide.region_0.1_spmd.sunk | while | flops 65541 | bytes 786547 | solution.py:19
  598.6 1.0 bitcast_add_fusion.2
  599.6 1.0 bitcast_add_fusion.2
  600.7 1.0 bitcast_add_fusion.2
  601.7 1.0 bitcast_add_fusion.2
  602.7 1.0 bitcast_add_fusion.2
  603.8 1.0 bitcast_add_fusion.2
  604.8 1.0 bitcast_add_fusion.2
  605.9 1.0 bitcast_add_fusion.2
  606.9 1.0 bitcast_add_fusion.2
  607.9 1.0 bitcast_add_fusion.2
  609.0 1.0 bitcast_add_fusion.2
  610.0 1.0 bitcast_add_fusion.2
  611.1 1.0 bitcast_add_fusion.2
  612.1 1.0 bitcast_add_fusion.2
  613.1 1.0 bitcast_add_fusion.2
  614.2 1.0 bitcast_add_fusion.2
  615.2 1.0 bitcast_add_fusion.2
  616.2 1.0 bitcast_add_fusion.2
  617.3 1.0 bitcast_add_fusion.2
  618.3 1.0 bitcast_add_fusion.2
  619.4 1.0 bitcast_add_fusion.2
  620.4 1.0 bitcast_add_fusion.2
  621.4 1.0 bitcast_add_fusion.2
  622.5 1.0 bitcast_add_fusion.2
  623.5 1.0 bitcast_add_fusion.2
  624.5 1.0 bitcast_add_fusion.2
  625.6 1.0 bitcast_add_fusion.2
  626.6 1.0 bitcast_add_fusion.2
  630.8 1.0 bitcast_add_fusion.2
  634.9 1.0 bitcast_add_fusion.2
  638.0 1.0 bitcast_add_fusion.2
  639.1 1.0 bitcast_add_fusion.2
  642.2 1.0 bitcast_add_fusion.2
  646.3 1.0 bitcast_add_fusion.2
  650.5 1.0 bitcast_add_fusion.2
  654.6 1.0 bitcast_add_fusion.2
  657.8 1.0 bitcast_add_fusion.2
  658.8 1.0 bitcast_add_fusion.2
  661.9 1.0 bitcast_add_fusion.2
  664.6 2.5 multiply_reduce_fusion
  (41 shorter events, 30.1 us)
Async XLA Ops:
  6.5 128.5 %all-gather.6.cloned.1.call-start = ((), (), s32[]{:S(2)}) async-start(), calls=%async_computation | async-start | bytes 4259840 | tf_op jit(solution)/shard_map/all_gather | solution.py:33
  7.3 255.4 %all-gather.8.cloned.1.call-start = ((), (), s32[]{:S(2)}) async-start(), calls=%async_computation.1 | async-start | bytes 4259840 | tf_op jit(solution)/shard_map/all_gather | solution.py:37
  8.0 382.4 %all-gather.10.cloned.1.call-start = ((), (), s32[]{:S(2)}) async-start(), calls=%async_computation.2 | async-start | bytes 4259840 | tf_op jit(solution)/shard_map/all_gather | solution.py:29
  8.7 589.8 %all-gather.12.cloned.1.call-start = ((), (), s32[]{:S(2)}) async-start(), calls=%async_computation.3 | async-start | bytes 17039360 | tf_op jit(solution)/shard_map/all_gather | solution.py:13
  268.5 0.8 copy-start
Sparse Core Ops, SparseCore 0:
  10.8 124.1 all-gather.5
  138.5 124.1 all-gather.7
  266.2 124.1 all-gather.9
  393.7 204.8 all-gather.11
where the time goes:
time: 677 us; the launch traced here: 675 us
  waiting for transfers between devices  572 us (84%)
  other arithmetic  63.9 us (9%)
  matrix products  21.6 us (3%)
  between operations  13.2 us (2%)
    all_gather x1, waiting for transfers between devices, carried_in(): gathered = lax.all_gather(part, axis)  202 us
    all_gather x1, waiting for transfers between devices, local(): lax.all_gather(w_key, 'ctx', axis=0, tiled=True)  126 us
    all_gather x1, waiting for transfers between devices, local(): lax.all_gather(w_value, 'ctx', axis=0, tiled=True)  122 us
    all_gather x1, waiting for transfers between devices, local(): lax.all_gather(w_query, 'ctx', axis=0, tiled=True)  120 us
    add x63, other arithmetic, add_states(): return earlier + later_part  63.7 us
  transfers between devices with their start and end apart: 4, of which 4 were waited for; matrix products, arithmetic and copies ran while one was open for 3% of the time, Pallas kernels for 0%

commit v1 on v0

--- a/solution.py
+++ b/solution.py
@@ -30,7 +30,11 @@
         preferred_element_type=jnp.float32,
     )
     key_full = jnp.dot(
-        tokens, lax.all_gather(w_key, "ctx", axis=0, tiled=True), preferred_element_type=jnp.float32
+        tokens,
+        jnp.concatenate(
+            lax.all_to_all(jnp.stack(lax.axis_size("ctx") * [w_key], axis=0), "ctx", 0, 0), axis=0
+        ),
+        preferred_element_type=jnp.float32,
     )
     value_full = jnp.dot(
         tokens,

time: 677 us -> 569 us (0.84)
  waiting for transfers between devices: 572 us -> 449 us
  starting transfers between devices: 0.12 us -> 11.7 us
    all_gather x1 -> x0, waiting for transfers between devices: 126 us -> none  [local(): lax.all_gather(w_key, 'ctx', axis=0, tiled=True)]
    all_to_all x0 -> x1, waiting for transfers between devices: none -> 101 us  [local(): lax.all_to_all(jnp.stack(lax.axis_size('ctx') * [w_key], axis=0), 'ctx',...]
    all_gather x1, waiting for transfers between devices: 122 us -> 23.2 us  [local(): lax.all_gather(w_value, 'ctx', axis=0, tiled=True)]
    all_to_all x0 -> x1, starting transfers between devices: none -> 11.6 us  [local(): lax.all_to_all(jnp.stack(lax.axis_size('ctx') * [w_key], axis=0), 'ctx',...]
  transfers between devices with their start and end apart: 4 -> 4, of which waited for: 4 -> 4; matrix products, arithmetic and copies ran while one was open for 3% -> 4% of each run, Pallas kernels for 0% -> 0%
where the time goes in v1:
time: 569 us; the launch traced here: 567 us
  waiting for transfers between devices  449 us (79%)
  other arithmetic  63.9 us (11%)
  matrix products  21.7 us (4%)
  between operations  13.2 us (2%)
  starting transfers between devices  11.7 us (2%)
    all_gather x1, waiting for transfers between devices, carried_in(): gathered = lax.all_gather(part, axis)  203 us
    all_gather x1, waiting for transfers between devices, local(): lax.all_gather(w_query, 'ctx', axis=0, tiled=True)  121 us
    all_to_all x1, waiting for transfers between devices, local(): lax.all_to_all(jnp.stack(lax.axis_size('ctx') * [w_key], axis=0), 'ctx',...  101 us
    add x63, other arithmetic, add_states(): return earlier + later_part  63.7 us
    all_gather x1, waiting for transfers between devices, local(): lax.all_gather(w_value, 'ctx', axis=0, tiled=True)  23.2 us
    all_to_all x1, starting transfers between devices, local(): lax.all_to_all(jnp.stack(lax.axis_size('ctx') * [w_key], axis=0), 'ctx',...  11.6 us
  transfers between devices with their start and end apart: 4, of which 4 were waited for; matrix products, arithmetic and copies ran while one was open for 4% of the time, Pallas kernels for 0%

profile of v1, /device:TPU:254, one launch (start us, length us, event | category | flops | bytes accessed | tf_op | source)
XLA Modules:
  0.0 566.6 jit_solution(807263348547113832)
XLA Ops:
  7.3 3.3 stack.2
  10.6 11.6 %all-to-all-start = ((bf16[64,64,512]{2,1,0:T(8,128)(2,1)}), bf16[64,64,512]{2,1,0:T(8,128)(2,1)}, u32[]{:S(2)}, u32[]{:S(2)}) async-start(bf16[64,64,512]{2,1,0:T(8,128)(2,1)} %stack.2), calls=%async_computation | async-start | bytes 8388608 | tf_op jit(solution)/shard_map/all_to_all | solution.py:35
  23.0 101.5 %all-to-all-done = bf16[64,64,512]{2,1,0:T(8,128)(2,1)} async-done(((bf16[64,64,512]{2,1,0:T(8,128)(2,1)}), bf16[64,64,512]{2,1,0:T(8,128)(2,1)}, u32[]{:S(2)}, u32[]{:S(2)}) %all-to-all-start) | async-done | bytes 4194336 | tf_op jit(solution)/shard_map/all_to_all | solution.py:35
  124.5 5.9 %convolution_convert_fusion.2 = bf16[512,512]{0,1:T(8,128)(2,1)S(1)} fusion(bf16[512,4096]{1,0:T(8,128)(2,1)} %param.6, bf16[4096,512]{1,0:T(8,128)(2,1)} %bitcast.1), kind=kOutput, calls=%fused_computation.7 | convolution fusion | flops 2147745792 | bytes 8912896 | tf_op jit(solution)/shard_map/dot_general | solution.py:32
  130.3 23.2 %all-gather.5.cloned.1.call-done = bf16[4096,512]{1,0:T(8,128)(2,1)} async-done(((bf16[64,512]{1,0:T(8,128)(2,1)}), bf16[4096,512]{1,0:T(8,128)(2,1)}) %all-gather.5.cloned.1.call-update) | async-done | bytes 4194320 | tf_op jit(solution)/shard_map/all_gather | solution.py:41
  153.5 5.8 %convolution_convert_fusion.1 = bf16[512,512]{0,1:T(8,128)(2,1)S(1)} fusion(bf16[512,4096]{1,0:T(8,128)(2,1)} %param.6, bf16[4096,512]{1,0:T(8,128)(2,1)} %all-gather.5.cloned.1.call-done), kind=kOutput, calls=%fused_computation.6 | convolution fusion | flops 2147745792 | bytes 8912896 | tf_op jit(solution)/shard_map/dot_general | solution.py:39
  161.3 120.7 %all-gather.7.cloned.1.call-done = bf16[4096,512]{1,0:T(8,128)(2,1)} async-done(((bf16[64,512]{1,0:T(8,128)(2,1)}), bf16[4096,512]{1,0:T(8,128)(2,1)}) %all-gather.7.cloned.1.call-update) | async-done | bytes 4194320 | tf_op jit(solution)/shard_map/all_gather | solution.py:29
  282.0 5.8 %convolution_convert_fusion = bf16[512,512]{0,1:T(8,128)(2,1)S(1)} fusion(bf16[512,4096]{1,0:T(8,128)(2,1)} %param.6, bf16[4096,512]{1,0:T(8,128)(2,1)} %all-gather.7.cloned.1.call-done), kind=kOutput, calls=%fused_computation.5 | convolution fusion | flops 2147745792 | bytes 8912896 | tf_op jit(solution)/shard_map/dot_general | solution.py:27
  287.9 202.5 %all-gather.9.cloned.1.call-done = f32[256,128,128]{2,1,0:T(8,128)} async-done(((f32[4,128,128]{2,1,0:T(8,128)}), f32[256,128,128]{2,1,0:T(8,128)}) %all-gather.9.cloned.1.call-update) | async-done | bytes 16777232 | tf_op jit(solution)/shard_map/all_gather | solution.py:13
  490.4 65.4 %while.10 = (s32[]{:T(128)}, f32[4,128,128]{2,1,0:T(8,128)S(1)}, s32[]{:T(128)}, f32[64,4,128,128]{3,2,1,0:T(8,128)}, s32[]{:T(128)}, /*index=5*/s32[]{:T(128)}, s32[]{:T(128)}) while((s32[]{:T(128)}, f32[4,128,128]{2,1,0:T(8,128)S(1)}, s32[]{:T(128)}, f32[64,4,128,128]{3,2,1,0:T(8,128)}, s32[]{:T(128)}, /*index=5*/s32[]{:T(128)}, ...), condition=%wide.region_1.2_spmd, body=%wide.region_0.1_spmd.sunk | while | flops 65541 | bytes 786547 | solution.py:19
  490.4 1.0 bitcast_add_fusion.2
  491.5 1.0 bitcast_add_fusion.2
  492.5 1.0 bitcast_add_fusion.2
  493.5 1.0 bitcast_add_fusion.2
  494.6 1.0 bitcast_add_fusion.2
  495.6 1.0 bitcast_add_fusion.2
  496.7 1.0 bitcast_add_fusion.2
  497.7 1.0 bitcast_add_fusion.2
  498.7 1.0 bitcast_add_fusion.2
  499.8 1.0 bitcast_add_fusion.2
  500.8 1.0 bitcast_add_fusion.2
  501.8 1.0 bitcast_add_fusion.2
  502.9 1.0 bitcast_add_fusion.2
  503.9 1.0 bitcast_add_fusion.2
  505.0 1.0 bitcast_add_fusion.2
  506.0 1.0 bitcast_add_fusion.2
  507.0 1.0 bitcast_add_fusion.2
  508.1 1.0 bitcast_add_fusion.2
  509.1 1.0 bitcast_add_fusion.2
  510.1 1.0 bitcast_add_fusion.2
  511.2 1.0 bitcast_add_fusion.2
  512.2 1.0 bitcast_add_fusion.2
  513.3 1.0 bitcast_add_fusion.2
  514.3 1.0 bitcast_add_fusion.2
  515.3 1.0 bitcast_add_fusion.2
  518.5 1.0 bitcast_add_fusion.2
  522.6 1.0 bitcast_add_fusion.2
  525.7 1.0 bitcast_add_fusion.2
  526.8 1.0 bitcast_add_fusion.2
  529.9 1.0 bitcast_add_fusion.2
  534.0 1.0 bitcast_add_fusion.2
  538.2 1.0 bitcast_add_fusion.2
  542.3 1.0 bitcast_add_fusion.2
  545.4 1.0 bitcast_add_fusion.2
  546.5 1.0 bitcast_add_fusion.2
  549.6 1.0 bitcast_add_fusion.2
  553.7 1.0 bitcast_add_fusion.2
  556.4 2.5 multiply_reduce_fusion
  (41 shorter events, 31.4 us)
Async XLA Ops:
  6.5 147.0 %all-gather.5.cloned.1.call-start = ((), (), s32[]{:S(2)}) async-start(), calls=%async_computation.1 | async-start | bytes 4259840 | tf_op jit(solution)/shard_map/all_gather | solution.py:41
  10.6 113.9 %all-to-all-start = ((bf16[64,64,512]{2,1,0:T(8,128)(2,1)}), bf16[64,64,512]{2,1,0:T(8,128)(2,1)}, u32[]{:S(2)}, u32[]{:S(2)}) async-start(bf16[64,64,512]{2,1,0:T(8,128)(2,1)} %stack.2), calls=%async_computation | async-start | bytes 8388608 | tf_op jit(solution)/shard_map/all_to_all | solution.py:35
  22.2 259.9 %all-gather.7.cloned.1.call-start = ((), (), s32[]{:S(2)}) async-start(), calls=%async_computation.2 | async-start | bytes 4259840 | tf_op jit(solution)/shard_map/all_gather | solution.py:29
  22.9 467.5 %all-gather.9.cloned.1.call-start = ((), (), s32[]{:S(2)}) async-start(), calls=%async_computation.3 | async-start | bytes 17039360 | tf_op jit(solution)/shard_map/all_gather | solution.py:13
  159.4 0.8 copy-start
Sparse Core Ops, SparseCore 0:
  10.8 142.6 all-gather.4
  157.0 124.9 all-gather.6
  285.5 204.8 all-gather.8
